TPU v7x, 512 devices: a whole 4x4x16 slice. The times are simulated.
512 devices in a mesh: ctx: 64 (over x, z_lo, core), head: 8 (over y, z_hi).
Axes of the slice: x: 4, y: 4, z: 16 (z_hi: 2, z_lo: 8; z = z_hi * 8 + z_lo), core: 2. Of those that a mesh axis runs over, the one named last changes fastest.
Arguments:
- queries: bfloat16 [16384, 2048], P('ctx', 'head'), may hold values from -40 to 40
- keys: bfloat16 [16384, 2048], P('ctx', 'head'), may hold values from -4 to 4
- values: bfloat16 [16384, 2048], P('ctx', 'head'), may hold values from -5 to 5
- selected: int32 [16, 512, 3], P('head', 'ctx'), may hold values from 0 to 63, as said below
- out_weight: bfloat16 [2048, 2048], P(None, 'head'), may hold values from -0.125 to 0.125
Outputs:
- projected: bfloat16 [16384, 2048], P('ctx', 'head')
Inputs may be any that keep to these rules, and one draw needn't show every extreme that they name: `selected`: entry 0 of a tile's selection is its own block; entries 1 and 2 are two different earlier blocks, or both the own block where no earlier block is chosen for the tile (one earlier block and the own block in the second key block). For each head, the tiles of one key block name any one other block at most 2 times, and exactly 2 times for every block they name, from the third key block on.
All inputs are finite; a program needn't handle non-finite values.
Results may differ from a plain program's by a relative error of at most 0.0054.
Values may be sent and summed in bfloat16 or wider, within the bound.
No kernel may reach another device: no remote copies, remote signals or barrier semaphores. Data moves between devices by JAX's collectives and lax.ppermute only.
A program may use at most 64 MiB of HBM per device.

v0:
```python
import jax
import jax.numpy as jnp
from jax import lax
from jax.sharding import Mesh, PartitionSpec as P

CAP = 2
LANE_ROWS = 4
LSE_ROWS = 16


def split_bf16(x):
    hi = lax.reduce_precision(x, exponent_bits=8, mantissa_bits=7)
    rest = x - hi
    mid = lax.reduce_precision(rest, exponent_bits=8, mantissa_bits=7)
    lo = rest - mid
    return jnp.stack([hi, mid, lo]).astype(jnp.bfloat16)


def join_bf16(parts):
    parts = parts.astype(jnp.float32)
    return parts[0] + (parts[1] + parts[2])


def softmax_pv(scores, vals):
    top = jnp.max(scores, axis=-1)
    prob = jnp.exp(scores - top[..., None])
    total = jnp.sum(prob, axis=-1)
    part = jnp.einsum(
        "hrk,khd->hrd", prob.astype(jnp.bfloat16), vals, preferred_element_type=jnp.float32
    )
    return (part / total[..., None], top + jnp.log(total))


def local(queries, keys, values, selected, out_weight):
    heads_loc = selected.shape[0]
    tiles = selected.shape[1]
    tokens_here = queries.shape[0]
    width = queries.shape[1] // heads_loc
    tile_rows = tokens_here // tiles
    sources = lax.axis_size("ctx")
    mine = lax.axis_index("ctx")
    scale = width ** (-0.5)
    quer_three = queries.reshape(tokens_here, heads_loc, width)
    keys_three = keys.reshape(tokens_here, heads_loc, width)
    vals_three = values.reshape(tokens_here, heads_loc, width)
    pos = jnp.arange(tokens_here, dtype=jnp.int32)
    own_scores = (
        jnp.einsum("rhd,khd->hrk", quer_three, keys_three, preferred_element_type=jnp.float32)
        * scale
    )
    own_scores = jnp.where((pos[:, None] >= pos[None, :])[None], own_scores, jnp.float32(-1e30))
    own_out, own_lse = softmax_pv(own_scores, vals_three)
    own_out = own_out.reshape(heads_loc, tiles, tile_rows, width)
    own_lse = own_lse.reshape(heads_loc, tiles, tile_rows)
    picks = selected[:, :, 1:]
    valid = picks != mine
    target = jnp.where(valid, picks, sources)
    onehot = (target[..., None] == jnp.arange(sources, dtype=jnp.int32)).astype(jnp.int32)
    flat_hot = onehot.reshape(heads_loc, tiles * 2, sources)
    before = jnp.cumsum(flat_hot, axis=1) - flat_hot
    slot = jnp.sum(before * flat_hot, axis=-1).reshape(heads_loc, tiles, 2)
    query_src = jnp.transpose(
        quer_three.reshape(tiles, tile_rows, heads_loc, width), (2, 0, 1, 3)
    ).reshape(heads_loc, tiles, tile_rows * width)
    flat_slot = target * CAP + slot
    route = (flat_slot[..., None] == jnp.arange(sources * CAP, dtype=jnp.int32)).astype(
        jnp.bfloat16
    )
    send_q = jnp.einsum(
        "htep,htx->phx", route, query_src, preferred_element_type=jnp.float32
    ).astype(jnp.bfloat16)
    send_q = send_q.reshape(sources, CAP, heads_loc, tile_rows, width)
    got_rows = lax.all_to_all(send_q, "ctx", split_axis=0, concat_axis=0, tiled=True)
    got_q = jnp.transpose(got_rows, (2, 0, 1, 3, 4)).reshape(
        heads_loc, sources * CAP * tile_rows, width
    )
    got_scores = (
        jnp.einsum("hrd,khd->hrk", got_q, keys_three, preferred_element_type=jnp.float32) * scale
    )
    part, lse = softmax_pv(got_scores, vals_three)
    part = jnp.transpose(
        part.reshape(heads_loc, sources, CAP, tile_rows, width), (1, 2, 0, 3, 4)
    ).reshape(sources, CAP * heads_loc * tile_rows, width)
    pieces = split_bf16(lse.reshape(heads_loc, sources, CAP, tile_rows))
    pieces = jnp.concatenate(
        [pieces, jnp.zeros((LANE_ROWS - 3,) + pieces.shape[1:], pieces.dtype)], axis=0
    )
    lse_rows = jnp.transpose(pieces, (2, 3, 1, 0, 4)).reshape(
        sources, CAP * heads_loc, LANE_ROWS * tile_rows
    )
    rows_part = CAP * heads_loc * tile_rows
    pad = -(rows_part + CAP * heads_loc) % 16
    back = jnp.concatenate(
        [part.astype(jnp.bfloat16), lse_rows, jnp.zeros((sources, pad, width), jnp.bfloat16)],
        axis=1,
    )
    got_back = lax.all_to_all(back, "ctx", split_axis=0, concat_axis=0, tiled=True)
    got_out = got_back[:, :rows_part].reshape(sources * CAP, heads_loc, tile_rows, width)
    got_lse = got_back[:, rows_part : rows_part + CAP * heads_loc].reshape(
        sources * CAP, heads_loc, width
    )
    pick_out = jnp.einsum("htep,phrd->hterd", route, got_out, preferred_element_type=jnp.float32)
    pick_parts = jnp.einsum(
        "htep,phx->htex", route, got_lse, preferred_element_type=jnp.float32
    ).reshape(heads_loc, tiles, 2, LANE_ROWS, tile_rows)
    pick_lse = pick_parts[:, :, :, 0] + (pick_parts[:, :, :, 1] + pick_parts[:, :, :, 2])
    keep = valid[..., None]
    top = jnp.maximum(own_lse, jnp.max(jnp.where(keep, pick_lse, own_lse[:, :, None]), axis=2))
    own_w = jnp.exp(own_lse - top)
    pick_w = jnp.exp(jnp.where(keep, pick_lse - top[:, :, None], jnp.float32(-1e30)))
    numer = own_w[..., None] * own_out + jnp.sum(pick_w[..., None] * pick_out, axis=2)
    denom = own_w + jnp.sum(pick_w, axis=2)
    attention = jnp.transpose(numer / denom[..., None], (1, 2, 0, 3)).reshape(
        tokens_here, heads_loc * width
    )
    attention = attention.astype(jnp.bfloat16)
    pair = lax.axis_size("zh")
    mine_zh = lax.axis_index("zh")
    own_rows = lax.all_gather(attention, "y", axis=1, tiled=True)
    partner = lax.ppermute(attention, "zh", [(0, 1), (1, 0)])
    partner_rows = lax.all_gather(partner, "y", axis=1, tiled=True)
    groups = out_weight.reshape(-1, pair, heads_loc * width, out_weight.shape[1])
    own_w = lax.dynamic_index_in_dim(groups, mine_zh, axis=1, keepdims=False)
    partner_w = lax.dynamic_index_in_dim(groups, 1 - mine_zh, axis=1, keepdims=False)
    projected = jnp.dot(
        own_rows, own_w.reshape(-1, out_weight.shape[1]), preferred_element_type=jnp.float32
    ) + jnp.dot(
        partner_rows, partner_w.reshape(-1, out_weight.shape[1]), preferred_element_type=jnp.float32
    )
    return projected.astype(jnp.bfloat16)


def solution(mesh):
    ctx_n, head_n = mesh.devices.shape
    split = Mesh(mesh.devices.reshape(ctx_n, head_n // 2, 2), ("ctx", "y", "zh"))
    head = ("y", "zh")
    return jax.shard_map(
        local,
        mesh=split,
        in_specs=(
            P("ctx", head),
            P("ctx", head),
            P("ctx", head),
            P(head, "ctx", None),
            P(None, head),
        ),
        out_specs=P("ctx", head),
        check_vma=False,
    )
```

profile of v0, /device:TPU:2, one launch (start us, length us, event | category | flops | bytes accessed | tf_op | source)
XLA Modules:
  0.0 310.1 jit_solution(9879162235493104044)
XLA Ops:
  0.0 0.0 copy-start
  0.0 0.7 slice.18
  0.7 0.1 copy.102
  0.8 0.1 eq.29
  0.9 0.1 fusion.51
  1.0 0.2 select_reduce_fusion
  1.2 0.1 reshape.199
  1.3 0.1 copy.69
  1.4 0.6 copy-done.10
  2.0 0.1 convert_reduce_fusion
  2.0 0.9 reshape_reshape.3
  3.0 0.7 convolution_convert_fusion
  3.7 0.5 copy.109
  4.2 1.8 copy.71
  6.0 16.1 %all-to-all-start = ((bf16[64,2,2,32,128]{4,3,1,2,0:T(8,128)(2,1)}), bf16[64,2,2,32,128]{4,3,1,2,0:T(8,128)(2,1)S(1)}, u32[]{:S(2)}, u32[]{:S(2)}) async-start(bf16[64,2,2,32,128]{4,3,1,2,0:T(8,128)(2,1)} %copy.71), calls=%async_computation | async-start | bytes 4194304 | tf_op jit(solution)/shard_map/all_to_all | solution.py:73
  22.1 0.1 pad.3.clone
  22.2 94.5 %all-to-all-done = bf16[64,2,2,32,128]{4,3,1,2,0:T(8,128)(2,1)S(1)} async-done(((bf16[64,2,2,32,128]{4,3,1,2,0:T(8,128)(2,1)}), bf16[64,2,2,32,128]{4,3,1,2,0:T(8,128)(2,1)S(1)}, u32[]{:S(2)}, u32[]{:S(2)}) %all-to-all-start) | async-done | bytes 2097184 | tf_op jit(solution)/shard_map/all_to_all | solution.py:73
  116.7 0.5 copy.72
  117.2 0.0 copy-done
  117.2 1.3 multiply_reduce_fusion
  118.5 0.0 copy-start.1
  118.5 0.0 copy-start.12
  118.5 1.4 fusion
  119.9 1.8 copy-done.1
  121.7 0.2 add.91
  121.9 0.1 copy.77
  122.1 0.1 copy.80
  122.2 0.0 copy-done.12
  122.2 5.0 %fusion.2 = bf16[2,4096,128]{2,1,0:T(8,128)(2,1)S(1)} fusion(f32[2,4096,256]{1,2,0:T(8,128)} %copy-done.1, f32[2,4096]{1,0:T(2,128)S(1)} %get-tuple-element.17, f32[2,4096]{1,0:T(2,128)S(1)} %fusion, bf16[256,256]{1,0:T(8,128)(2,1)S(1)} %copy-done.12), kind=kOutput, calls=%fused_computation.6 | convolution fusion | flops 545259520 | bytes 10682368 | tf_op jit(solution)/shard_map/hrk,khd->hrd/dot_general | solution.py:28
  127.2 0.6 copy.76
  127.8 0.0 copy-start.6
  127.8 1.9 maximum_maximum_fusion
  129.7 9.8 %all-to-all-start.1 = ((bf16[64,144,128]{2,1,0:T(8,128)(2,1)}), bf16[64,144,128]{2,1,0:T(8,128)(2,1)S(1)}, u32[]{:S(2)}, u32[]{:S(2)}) async-start(bf16[64,144,128]{2,1,0:T(8,128)(2,1)} %maximum_maximum_fusion), calls=%async_computation.1 | async-start | bytes 4718592 | tf_op jit(solution)/shard_map/all_to_all | solution.py:97
  139.6 0.2 fusion.60
  139.9 0.8 copy-done.2
  140.7 0.1 fusion.17
  140.7 0.0 copy-start.9
  140.8 0.1 add.88
  140.9 0.1 copy.68
  141.0 0.4 copy-done.9
  141.3 1.3 constant_dynamic-slice_fusion.1
  142.6 2.1 convolution_divide_fusion.1
  144.7 100.3 %all-to-all-done.1 = bf16[64,144,128]{2,1,0:T(8,128)(2,1)S(1)} async-done(((bf16[64,144,128]{2,1,0:T(8,128)(2,1)}), bf16[64,144,128]{2,1,0:T(8,128)(2,1)S(1)}, u32[]{:S(2)}, u32[]{:S(2)}) %all-to-all-start.1) | async-done | bytes 2359328 | tf_op jit(solution)/shard_map/all_to_all | solution.py:97
  245.1 1.4 fusion.44
  246.6 1.4 reshape.206
  248.0 1.0 fusion.59
  249.0 0.1 fusion.46
  249.1 1.9 fusion.57
  251.0 1.4 copy.89
  252.5 1.3 fusion.56
  253.8 1.4 copy.85
  255.1 1.4 copy.91
  256.5 0.3 slice.28
  256.8 0.5 copy-done.7
  257.4 1.2 fusion.12
  258.6 0.0 copy-done.3
  258.6 0.2 fusion.38
  258.9 0.1 copy.92
  259.1 14.0 %all_gather.6 = bf16[256,1024]{1,0:T(8,128)(2,1)S(1)} all-gather(bf16[256,256]{1,0:T(8,128)(2,1)S(1)} %bitcast.112), channel_id=1, replica_groups=mesh['ctx'=64,'y'=4,'zh'=2] {'y'}, dimensions={1}, use_global_device_ids=true | all-gather | bytes 655360 | tf_op jit(solution)/shard_map/all_gather | solution.py:119
  273.1 8.2 %collective-permute-start = (bf16[256,256]{1,0:T(8,128)(2,1)S(1)}, bf16[256,256]{1,0:T(8,128)(2,1)S(1)}, u32[]{:S(2)}, u32[]{:S(2)}) collective-permute-start(bf16[256,256]{1,0:T(8,128)(2,1)S(1)} %bitcast.113), channel_id=1, source_target_pairs={{0,1},{1,0},{2,3},{3,2},{4,5},{5,4},{6,7},{7,6},{8,9},{9,8},{10,11... | collective-permute-start | bytes 393224 | tf_op jit(solution)/shard_map/ppermute | solution.py:120
  281.3 0.3 fusion.61
  281.6 14.2 %collective-permute-done = bf16[256,256]{1,0:T(8,128)(2,1)S(1)} collective-permute-done((bf16[256,256]{1,0:T(8,128)(2,1)S(1)}, bf16[256,256]{1,0:T(8,128)(2,1)S(1)}, u32[]{:S(2)}, u32[]{:S(2)}) %collective-permute-start) | collective-permute-done | bytes 131104 | tf_op jit(solution)/shard_map/ppermute | solution.py:120
  295.8 13.3 %all_gather.7 = bf16[256,1024]{1,0:T(8,128)(2,1)S(1)} all-gather(bf16[256,256]{1,0:T(8,128)(2,1)S(1)} %collective-permute-done), channel_id=1, replica_groups=mesh['ctx'=64,'y'=4,'zh'=2] {'y'}, dimensions={1}, use_global_device_ids=true | all-gather | bytes 655360 | tf_op jit(solution)/shard_map/all_gather | solution.py:121
  309.1 1.0 fusion.15
  (27 shorter events, 0.3 us)
Async XLA Ops:
  0.0 117.2 %copy-start = (bf16[256,256]{1,0:T(8,128)(2,1)S(1)}, bf16[256,256]{1,0:T(8,128)(2,1)}, u32[]{:S(2)}) copy-start(bf16[256,256]{1,0:T(8,128)(2,1)} %param.6) | copy-start | bytes 393220
  1.4 0.6 copy-start.10
  6.0 110.7 %all-to-all-start = ((bf16[64,2,2,32,128]{4,3,1,2,0:T(8,128)(2,1)}), bf16[64,2,2,32,128]{4,3,1,2,0:T(8,128)(2,1)S(1)}, u32[]{:S(2)}, u32[]{:S(2)}) async-start(bf16[64,2,2,32,128]{4,3,1,2,0:T(8,128)(2,1)} %copy.71), calls=%async_computation | async-start | bytes 4194304 | tf_op jit(solution)/shard_map/all_to_all | solution.py:73
  118.5 3.2 %copy-start.1 = (f32[2,4096,256]{1,2,0:T(8,128)}, f32[2,4096,256]{1,2,0:T(8,128)S(1)}, u32[]{:S(2)}) copy-start(f32[2,4096,256]{1,2,0:T(8,128)S(1)} %get-tuple-element.18) | copy-start | bytes 25165828
  118.5 3.7 %copy-start.12 = (bf16[256,256]{1,0:T(8,128)(2,1)S(1)}, bf16[256,256]{1,0:T(8,128)(2,1)}, u32[]{:S(2)}) copy-start(bf16[256,256]{1,0:T(8,128)(2,1)} %param.7) | copy-start | bytes 393220
  127.8 11.8 %copy-start.6 = (bf16[256,256]{1,0:T(8,128)(2,1)S(1)}, bf16[256,256]{1,0:T(8,128)(2,1)}, u32[]{:S(2)}) copy-start(bf16[256,256]{1,0:T(8,128)(2,1)} %param.5) | copy-start | bytes 393220
  129.7 115.3 %all-to-all-start.1 = ((bf16[64,144,128]{2,1,0:T(8,128)(2,1)}), bf16[64,144,128]{2,1,0:T(8,128)(2,1)S(1)}, u32[]{:S(2)}, u32[]{:S(2)}) async-start(bf16[64,144,128]{2,1,0:T(8,128)(2,1)} %maximum_maximum_fusion), calls=%async_computation.1 | async-start | bytes 4718592 | tf_op jit(solution)/shard_map/all_to_all | solution.py:97
  139.8 0.8 copy-start.2
  140.7 0.6 copy-start.9
  141.0 108.0 %copy-start.8 = (pred[2,8,2]{1,2,0:T(4,128)(4,1)}, pred[2,8,2]{1,2,0:T(4,128)(4,1)S(1)}, u32[]{:S(2)}) copy-start(pred[2,8,2]{1,2,0:T(4,128)(4,1)S(1)} %copy.68) | copy-start | bytes 100
  253.8 3.1 copy-start.11
  256.5 0.8 copy-start.7
  256.5 2.1 copy-start.3
  256.5 2.1 copy-start.4
  256.5 2.1 copy-start.5
  273.1 22.7 %collective-permute-start = (bf16[256,256]{1,0:T(8,128)(2,1)S(1)}, bf16[256,256]{1,0:T(8,128)(2,1)S(1)}, u32[]{:S(2)}, u32[]{:S(2)}) collective-permute-start(bf16[256,256]{1,0:T(8,128)(2,1)S(1)} %bitcast.113), channel_id=1, source_target_pairs={{0,1},{1,0},{2,3},{3,2},{4,5},{5,4},{6,7},{7,6},{8,9},{9,8},{10,11... | collective-permute-start | bytes 393224 | tf_op jit(solution)/shard_map/ppermute | solution.py:120
where the time goes:
time: 311 us; the launch traced here: 310 us
  waiting for transfers between devices  209 us (67%)
  starting transfers between devices  34.1 us (11%)
  blocking collectives  27.3 us (9%)
  local copies, waits for them, and re-layouts  18.4 us (6%)
  matrix products  13.4 us (4%)
  other arithmetic  7.55 us (2%)
    all_to_all x1, waiting for transfers between devices, local(): lax.all_to_all(back, 'ctx', split_axis=0, concat_axis=0, tiled=True)  100 us
    all_to_all x1, waiting for transfers between devices, local(): lax.all_to_all(send_q, 'ctx', split_axis=0, concat_axis=0, tiled=True)  94.5 us
    all_to_all x1, starting transfers between devices, local(): lax.all_to_all(send_q, 'ctx', split_axis=0, concat_axis=0, tiled=True)  16.1 us
    ppermute x1, waiting for transfers between devices, local(): partner = lax.ppermute(attention, 'zh', [(0, 1), (1, 0)])  14.2 us
    all_gather x1, blocking collectives, local(): own_rows = lax.all_gather(attention, 'y', axis=1, tiled=True)  14 us
    all_gather x1, blocking collectives, local(): partner_rows = lax.all_gather(partner, 'y', axis=1, tiled=True)  13.3 us
    all_to_all x1, starting transfers between devices, local(): lax.all_to_all(back, 'ctx', split_axis=0, concat_axis=0, tiled=True)  9.81 us
    ppermute x1, starting transfers between devices, local(): partner = lax.ppermute(attention, 'zh', [(0, 1), (1, 0)])  8.2 us
  transfers between devices with their start and end apart: 3, of which 3 were waited for; matrix products, arithmetic and copies ran while one was open for 1% of the time, Pallas kernels for 0%

commit v1 on v0

--- a/solution.py
+++ b/solution.py
@@ -1,3 +1,4 @@
+import functools
 import jax
 import jax.numpy as jnp
 from jax import lax
@@ -6,6 +7,15 @@
 CAP = 2
 LANE_ROWS = 4
 LSE_ROWS = 16
+
+
+def detail_values(x0, axis_id):
+    mixed_arr = jnp.stack(jax.lax.axis_size(axis_id) * [x0])
+    tall = jax.lax.all_to_all(mixed_arr, axis_name=axis_id, split_axis=0, concat_axis=0)
+    return jnp.concatenate(tall, axis=1)
+
+
+perform_rows = functools.partial(detail_values, axis_id="y")
 
 
 def split_bf16(x):
@@ -116,7 +126,7 @@
     attention = attention.astype(jnp.bfloat16)
     pair = lax.axis_size("zh")
     mine_zh = lax.axis_index("zh")
-    own_rows = lax.all_gather(attention, "y", axis=1, tiled=True)
+    own_rows = perform_rows(attention)
     partner = lax.ppermute(attention, "zh", [(0, 1), (1, 0)])
     partner_rows = lax.all_gather(partner, "y", axis=1, tiled=True)
     groups = out_weight.reshape(-1, pair, heads_loc * width, out_weight.shape[1])

time: 311 us -> 296 us (0.952)
  the two profiles are of different devices: /device:TPU:2 before, /device:TPU:14 now
where the time goes in v1:
time: 296 us
  waiting for transfers between devices  215 us (73%)
  starting transfers between devices  39.1 us (13%)
  blocking collectives  13.4 us (5%)
  local copies, waits for them, and re-layouts  12 us (4%)
  matrix products  11 us (4%)
  other arithmetic  4.41 us (1%)
    all_to_all x1, waiting for transfers between devices, local(): lax.all_to_all(back, 'ctx', split_axis=0, concat_axis=0, tiled=True)  104 us
    all_to_all x1, waiting for transfers between devices, local(): lax.all_to_all(send_q, 'ctx', split_axis=0, concat_axis=0, tiled=True)  94.5 us
    ppermute x1, waiting for transfers between devices, local(): partner = lax.ppermute(attention, 'zh', [(0, 1), (1, 0)])  17 us
    all_to_all x1, starting transfers between devices, local(): lax.all_to_all(send_q, 'ctx', split_axis=0, concat_axis=0, tiled=True)  16.2 us
    all_gather x1, blocking collectives, local(): partner_rows = lax.all_gather(partner, 'y', axis=1, tiled=True)  13.4 us
    all_to_all x1, starting transfers between devices, local(): lax.all_to_all(back, 'ctx', split_axis=0, concat_axis=0, tiled=True)  9.79 us
    ppermute x1, starting transfers between devices, local(): partner = lax.ppermute(attention, 'zh', [(0, 1), (1, 0)])  8.21 us
    dot_general x2, matrix products, softmax_pv(): jnp.einsum('hrk,khd->hrd', prob.astype(jnp.bfloat16), vals, preferred_ele...  6.02 us
  transfers between devices with their start and end apart: 4, of which 3 were waited for; matrix products, arithmetic and copies ran while one was open for 1% of the time, Pallas kernels for 0%

profile of v1, /device:TPU:14, one launch (start us, length us, event | category | flops | bytes accessed | tf_op | source)
XLA Modules:
  0.0 295.8 jit_solution(5433428052232075533)
XLA Ops:
  0.0 0.0 copy-start
  0.0 0.7 slice.18
  0.7 0.1 copy.105
  0.8 0.1 eq.29
  0.9 0.1 fusion.51
  1.0 0.2 select_reduce_fusion
  1.2 0.1 reshape.208
  1.3 0.1 copy.71
  1.4 0.1 convert_reduce_fusion
  1.5 1.0 reshape_reshape.3
  2.4 0.7 convolution_convert_fusion
  3.2 0.5 copy.112
  3.6 1.8 copy.73
  5.5 16.2 %all-to-all-start = ((bf16[64,2,2,32,128]{4,3,1,2,0:T(8,128)(2,1)}), bf16[64,2,2,32,128]{4,3,1,2,0:T(8,128)(2,1)S(1)}, u32[]{:S(2)}, u32[]{:S(2)}) async-start(bf16[64,2,2,32,128]{4,3,1,2,0:T(8,128)(2,1)} %copy.73), calls=%async_computation | async-start | bytes 4194304 | tf_op jit(solution)/shard_map/all_to_all | solution.py:83
  21.7 0.1 pad.3.clone
  21.8 94.5 %all-to-all-done = bf16[64,2,2,32,128]{4,3,1,2,0:T(8,128)(2,1)S(1)} async-done(((bf16[64,2,2,32,128]{4,3,1,2,0:T(8,128)(2,1)}), bf16[64,2,2,32,128]{4,3,1,2,0:T(8,128)(2,1)S(1)}, u32[]{:S(2)}, u32[]{:S(2)}) %all-to-all-start) | async-done | bytes 2097184 | tf_op jit(solution)/shard_map/all_to_all | solution.py:83
  116.3 0.5 copy.74
  116.8 0.0 copy-done
  116.8 1.3 multiply_reduce_fusion
  118.1 0.0 copy-start.1
  118.1 0.0 copy-start.8
  118.1 1.4 fusion
  119.5 1.8 copy-done.1
  121.3 0.2 add.91
  121.5 0.1 copy.79
  121.7 0.1 copy.82
  121.8 0.0 copy-done.8
  121.8 5.0 %fusion.2 = bf16[2,4096,128]{2,1,0:T(8,128)(2,1)S(1)} fusion(f32[2,4096,256]{1,2,0:T(8,128)} %copy-done.1, f32[2,4096]{1,0:T(2,128)S(1)} %get-tuple-element.17, f32[2,4096]{1,0:T(2,128)S(1)} %fusion, bf16[256,256]{1,0:T(8,128)(2,1)S(1)} %copy-done.8), kind=kOutput, calls=%fused_computation.6 | convolution fusion | flops 545259520 | bytes 10682368 | tf_op jit(solution)/shard_map/hrk,khd->hrd/dot_general | solution.py:38
  126.8 0.6 copy.78
  127.4 0.0 copy-start.6
  127.4 1.9 maximum_maximum_fusion
  129.3 9.8 %all-to-all-start.1 = ((bf16[64,144,128]{2,1,0:T(8,128)(2,1)}), bf16[64,144,128]{2,1,0:T(8,128)(2,1)S(1)}, u32[]{:S(2)}, u32[]{:S(2)}) async-start(bf16[64,144,128]{2,1,0:T(8,128)(2,1)} %maximum_maximum_fusion), calls=%async_computation.1 | async-start | bytes 4718592 | tf_op jit(solution)/shard_map/all_to_all | solution.py:107
  139.2 0.0 copy-done.6
  139.2 0.2 fusion.60
  139.4 0.1 fusion.17
  139.5 0.1 add.88
  139.6 0.1 copy.70
  139.7 1.0 convolution_divide_fusion.1
  140.7 103.9 %all-to-all-done.1 = bf16[64,144,128]{2,1,0:T(8,128)(2,1)S(1)} async-done(((bf16[64,144,128]{2,1,0:T(8,128)(2,1)}), bf16[64,144,128]{2,1,0:T(8,128)(2,1)S(1)}, u32[]{:S(2)}, u32[]{:S(2)}) %all-to-all-start.1) | async-done | bytes 2359328 | tf_op jit(solution)/shard_map/all_to_all | solution.py:107
  244.7 0.2 fusion.44
  244.9 0.1 reshape.215
  245.0 0.1 fusion.46
  245.1 0.1 fusion.57
  245.2 0.7 copy.91
  245.9 0.7 copy.87
  246.6 0.7 copy.93
  247.3 0.0 copy-start.2
  247.3 0.3 slice.28
  247.6 0.5 copy-done.7
  248.1 1.2 fusion.12
  249.4 0.0 copy-done.3
  249.4 0.0 copy-done.4
  249.4 0.2 fusion.38
  249.7 0.1 copy.94
  249.8 0.1 copy.95
  249.9 0.8 stack.6
  250.8 4.9 %all-to-all-start.2 = ((bf16[4,256,256]{1,2,0:T(8,128)(2,1)}), bf16[4,256,256]{1,2,0:T(8,128)(2,1)S(1)}, u32[]{:S(2)}, u32[]{:S(2)}) async-start(bf16[4,256,256]{1,2,0:T(8,128)(2,1)} %stack.6), calls=%async_computation.2 | async-start | bytes 1048576 | tf_op jit(solution)/shard_map/all_to_all | solution.py:14
  255.7 8.2 %collective-permute-start = (bf16[256,256]{1,0:T(8,128)(2,1)S(1)}, bf16[256,256]{1,0:T(8,128)(2,1)S(1)}, u32[]{:S(2)}, u32[]{:S(2)}) collective-permute-start(bf16[256,256]{1,0:T(8,128)(2,1)S(1)} %bitcast.118), channel_id=1, source_target_pairs={{0,1},{1,0},{2,3},{3,2},{4,5},{5,4},{6,7},{7,6},{8,9},{9,8},{10,11... | collective-permute-start | bytes 393224 | tf_op jit(solution)/shard_map/ppermute | solution.py:130
  263.9 0.1 constant_dynamic-slice_fusion.1
  264.0 17.0 %collective-permute-done = bf16[256,256]{1,0:T(8,128)(2,1)S(1)} collective-permute-done((bf16[256,256]{1,0:T(8,128)(2,1)S(1)}, bf16[256,256]{1,0:T(8,128)(2,1)S(1)}, u32[]{:S(2)}, u32[]{:S(2)}) %collective-permute-start) | collective-permute-done | bytes 131104 | tf_op jit(solution)/shard_map/ppermute | solution.py:130
  281.0 13.4 %all_gather.3 = bf16[256,1024]{1,0:T(8,128)(2,1)S(1)} all-gather(bf16[256,256]{1,0:T(8,128)(2,1)S(1)} %collective-permute-done), channel_id=1, replica_groups=mesh['ctx'=64,'y'=4,'zh'=2] {'y'}, dimensions={1}, use_global_device_ids=true | all-gather | bytes 655360 | tf_op jit(solution)/shard_map/all_gather | solution.py:131
  294.4 0.0 all-to-all-done.2
  294.4 0.3 fusion.61
  294.8 1.0 fusion.15
  (22 shorter events, 0.3 us)
Async XLA Ops:
  0.0 116.8 %copy-start = (bf16[256,256]{1,0:T(8,128)(2,1)S(1)}, bf16[256,256]{1,0:T(8,128)(2,1)}, u32[]{:S(2)}) copy-start(bf16[256,256]{1,0:T(8,128)(2,1)} %param.6) | copy-start | bytes 393220
  5.5 110.8 %all-to-all-start = ((bf16[64,2,2,32,128]{4,3,1,2,0:T(8,128)(2,1)}), bf16[64,2,2,32,128]{4,3,1,2,0:T(8,128)(2,1)S(1)}, u32[]{:S(2)}, u32[]{:S(2)}) async-start(bf16[64,2,2,32,128]{4,3,1,2,0:T(8,128)(2,1)} %copy.73), calls=%async_computation | async-start | bytes 4194304 | tf_op jit(solution)/shard_map/all_to_all | solution.py:83
  118.1 3.2 %copy-start.1 = (f32[2,4096,256]{1,2,0:T(8,128)}, f32[2,4096,256]{1,2,0:T(8,128)S(1)}, u32[]{:S(2)}) copy-start(f32[2,4096,256]{1,2,0:T(8,128)S(1)} %get-tuple-element.18) | copy-start | bytes 25165828
  118.1 3.7 %copy-start.8 = (bf16[256,256]{1,0:T(8,128)(2,1)S(1)}, bf16[256,256]{1,0:T(8,128)(2,1)}, u32[]{:S(2)}) copy-start(bf16[256,256]{1,0:T(8,128)(2,1)} %param.7) | copy-start | bytes 393220
  127.4 11.8 %copy-start.6 = (bf16[256,256]{1,0:T(8,128)(2,1)S(1)}, bf16[256,256]{1,0:T(8,128)(2,1)}, u32[]{:S(2)}) copy-start(bf16[256,256]{1,0:T(8,128)(2,1)} %param.5) | copy-start | bytes 393220
  129.3 115.3 %all-to-all-start.1 = ((bf16[64,144,128]{2,1,0:T(8,128)(2,1)}), bf16[64,144,128]{2,1,0:T(8,128)(2,1)S(1)}, u32[]{:S(2)}, u32[]{:S(2)}) async-start(bf16[64,144,128]{2,1,0:T(8,128)(2,1)} %maximum_maximum_fusion), calls=%async_computation.1 | async-start | bytes 4718592 | tf_op jit(solution)/shard_map/all_to_all | solution.py:107
  247.3 0.8 copy-start.7
  247.3 2.1 copy-start.3
  247.3 2.1 copy-start.4
  247.3 2.1 copy-start.5
  247.3 16.6 %copy-start.2 = (bf16[2048,256]{1,0:T(8,128)(2,1)S(1)}, bf16[2048,256]{1,0:T(8,128)(2,1)}, u32[]{:S(2)}) copy-start(bf16[2048,256]{1,0:T(8,128)(2,1)} %param.9) | copy-start | bytes 3145732
  250.8 43.7 %all-to-all-start.2 = ((bf16[4,256,256]{1,2,0:T(8,128)(2,1)}), bf16[4,256,256]{1,2,0:T(8,128)(2,1)S(1)}, u32[]{:S(2)}, u32[]{:S(2)}) async-start(bf16[4,256,256]{1,2,0:T(8,128)(2,1)} %stack.6), calls=%async_computation.2 | async-start | bytes 1048576 | tf_op jit(solution)/shard_map/all_to_all | solution.py:14
  255.7 25.3 %collective-permute-start = (bf16[256,256]{1,0:T(8,128)(2,1)S(1)}, bf16[256,256]{1,0:T(8,128)(2,1)S(1)}, u32[]{:S(2)}, u32[]{:S(2)}) collective-permute-start(bf16[256,256]{1,0:T(8,128)(2,1)S(1)} %bitcast.118), channel_id=1, source_target_pairs={{0,1},{1,0},{2,3},{3,2},{4,5},{5,4},{6,7},{7,6},{8,9},{9,8},{10,11... | collective-permute-start | bytes 393224 | tf_op jit(solution)/shard_map/ppermute | solution.py:130
